TPU v7x, 32 devices: a whole 2x2x4 slice. The times are simulated.
32 devices in a mesh: swath: 2 (over y), sub: 4 (over z), beam: 2 (over x), half: 2 (over core).
Axes of the slice: x: 2, y: 2, z: 4, core: 2. Of those that a mesh axis runs over, the one named last changes fastest.
Arguments:
- images: bfloat16 [4, 2, 2048, 1024], P('sub', None, ('swath', 'half'), 'beam'), parts along dimension 2, may hold values from -6 to 6
- offsets: float32 [4], replicated, may hold values from 3840 to 4505
- owners: int32 [2, 4], replicated, may hold values from 0 to 3, each once within a row
Outputs:
- sectors: bfloat16 [8, 1, 2, 512, 2048], P(('sub', 'beam'), None, None, None, ('swath', 'half')), parts along dimension 4
There are 2 independent parts, one for each index of `swath`. A program takes and returns all parts, laid end to end along the dimension named above; an argument that names none is the same for every part. Nothing has to cross between parts.
Inputs may be any that keep to these rules, and one draw needn't show every extreme that they name: Each row of owners names every one of the 4 sectors of its beam shard exactly once.
All inputs are finite; a program needn't handle non-finite values.
Results may differ from a plain program's by a relative error of at most 0.0052.
Values may be sent and summed in bfloat16 or wider, within the bound.
No kernel may reach another device: no remote copies, remote signals or barrier semaphores. Data moves between devices by JAX's collectives and lax.ppermute only.
A program may use at most 64 MiB of HBM per device.

v0:
```python
import math
import jax
import numpy as np
import jax.numpy as jnp
from jax import lax
from jax.sharding import PartitionSpec as P

B = 1024
NR = 1024


def swapped(value, axis, distance):
    return lax.ppermute(value, axis, [(i, i ^ 1 << distance) for i in range(lax.axis_size(axis))])


def odd_kernel(beam_total, columns):
    spacing = (
        np.arange(columns, dtype=np.int64)[None, :] - np.arange(beam_total, dtype=np.int64)[:, None]
    )
    parity = np.where(spacing % 2 == 0, 1.0, -1.0).astype(np.float32)
    angles = (2.0 * spacing.astype(np.float32) + np.float32(1.0)) * np.float32(
        math.pi / (2.0 * beam_total)
    )
    values = parity * np.cos(angles) / (np.float32(beam_total) * np.sin(angles))
    return jnp.asarray(values.astype(np.float32).astype(jnp.bfloat16))


def steer_phase(upsampled, shifts, rows_at, beams_at, beams_out):
    ratios = NR / (NR + rows_at.astype(jnp.float32))
    tilts = (2.0 * beams_at.astype(jnp.float32) + 1.0) / beams_out - 1.0
    phases = ratios[:, None] * tilts[None, :] * shifts[..., None, None]
    cosine = jnp.cos(phases)
    sines = jnp.sin(phases)
    real_part = upsampled[..., 0, :, :]
    imag_part = upsampled[..., 1, :, :]
    return jnp.stack(
        [real_part * cosine - imag_part * sines, real_part * sines + imag_part * cosine], -3
    )


def rotate_sum(children, odd_beams, shifts, rows_at, beams_out):
    count = children.shape[-1]
    even_at = 2 * jnp.arange(count, dtype=jnp.int32)
    even_sum = jnp.sum(
        steer_phase(children.astype(jnp.float32), shifts, rows_at, even_at, beams_out), axis=0
    )
    odd_sum = jnp.sum(steer_phase(odd_beams, shifts, rows_at, even_at + 1, beams_out), axis=0)
    joined = jnp.stack([even_sum, odd_sum], -1)
    return joined.reshape(even_sum.shape[:-1] + (2 * count,)).astype(jnp.bfloat16)


def odd_local(children, kernel):
    product = jnp.dot(
        children.reshape(-1, children.shape[-1]), kernel, preferred_element_type=jnp.float32
    )
    return product.reshape(children.shape[:-1] + (kernel.shape[1],))


def swap_first(pieces):
    return swapped(pieces, "sub", 0)


def swap_second(pieces):
    return swapped(pieces, "sub", 1)


def keep_and_trade(field, which_bit, swapper):
    length = field.shape[2] // 2
    kept = lax.dynamic_slice_in_dim(field, which_bit * length, length, 2)
    given = lax.dynamic_slice_in_dim(field, (1 - which_bit) * length, length, 2)
    return (jnp.stack([kept, swapper(given)]), length)


def shift_block(offsets, index, per_device):
    return lax.dynamic_slice_in_dim(offsets, index * per_device, per_device, 0)


def body(images, offsets, owners):
    sub_count = lax.axis_size("sub")
    beam_count = lax.axis_size("beam")
    sub_place = lax.axis_index("sub")
    beam_lane = lax.axis_index("beam")
    half_side = lax.axis_index("half")
    low_bit = sub_place % 2
    high_bit = sub_place // 2 % 2
    per_device = images.shape[0]
    half_rows = images.shape[2]
    own_shift = shift_block(offsets, sub_place, per_device)
    mate_shift = shift_block(offsets, jnp.bitwise_xor(sub_place, 1), per_device)
    shifts_one = jnp.stack([own_shift, mate_shift])
    pair_base = sub_place - low_bit
    mate_base = jnp.bitwise_xor(sub_place, 2) - low_bit
    center_own = (
        shift_block(offsets, pair_base, per_device)
        + shift_block(offsets, pair_base + 1, per_device)
    ) * 0.5
    center_mate = (
        shift_block(offsets, mate_base, per_device)
        + shift_block(offsets, mate_base + 1, per_device)
    ) * 0.5
    shifts_two = jnp.stack([center_own, center_mate])
    all_beams = lax.all_to_all(images, "beam", split_axis=2, concat_axis=3, tiled=True)
    block_rows = all_beams.shape[2]
    start_row = half_side * half_rows + beam_lane * block_rows
    children, length = keep_and_trade(all_beams, low_bit, swap_first)
    rows_at = start_row + low_bit * length + jnp.arange(length, dtype=jnp.int32)
    odd_beams = odd_local(children, odd_kernel(B, B))
    first_merge = rotate_sum(children, odd_beams, shifts_one, rows_at, 2 * B)
    children, quarter = keep_and_trade(first_merge, high_bit, swap_second)
    rows_at = (
        start_row + low_bit * length + high_bit * quarter + jnp.arange(quarter, dtype=jnp.int32)
    )
    odd_beams = odd_local(children, odd_kernel(2 * B, 2 * B))
    merged = rotate_sum(children, odd_beams, shifts_two, rows_at, 4 * B)
    sector_tiles = merged.reshape(per_device, 2, quarter, beam_count, sub_count, -1)
    beam_ids = jnp.arange(beam_count, dtype=jnp.int32)[:, None]
    picked = sector_tiles[:, :, :, beam_ids, owners, :]
    outgoing = picked.transpose(4, 3, 0, 1, 5, 2)
    received = lax.all_to_all(
        lax.all_to_all(outgoing, "sub", split_axis=0, concat_axis=0, tiled=True),
        "beam",
        split_axis=1,
        concat_axis=1,
        tiled=True,
    )
    sector_width = received.shape[4]
    received = received.reshape(
        sub_count // 4, 2, 2, beam_count, per_device, 2, sector_width, quarter
    )
    received = received.transpose(0, 4, 5, 6, 3, 2, 1, 7)
    return received.reshape(1, sub_count // 4 * per_device, 2, sector_width, half_rows)


def solution(mesh):
    placed = (P("sub", None, ("swath", "half"), "beam"), P(), P())
    return jax.shard_map(
        body,
        mesh=mesh,
        in_specs=placed,
        out_specs=P(("sub", "beam"), None, None, None, ("swath", "half")),
        check_vma=False,
    )
```

profile of v0, /device:TPU:0, one launch (start us, length us, event | category | flops | bytes accessed | tf_op | source)
XLA Modules:
  0.0 138.8 jit_solution(17803852248841441353)
XLA Ops:
  0.0 0.0 copy-start
  0.0 3.3 %copy.34 = bf16[1,2,512,512]{3,1,0,2:T(2,128)(2,1)} copy(bf16[1,2,512,512]{3,2,1,0:T(8,128)(2,1)} %param.5) | data formatting | bytes 2097152 | tf_op args[0]
  3.3 4.2 %all-to-all-start = ((bf16[1,2,512,512]{3,1,0,2:T(2,128)(2,1)}), bf16[1,2,512,512]{3,1,0,2:T(2,128)(2,1)S(1)}, u32[]{:S(2)}, u32[]{:S(2)}) async-start(bf16[1,2,512,512]{3,1,0,2:T(2,128)(2,1)} %copy.34), calls=%async_computation | async-start | bytes 2097152 | tf_op jit(solution)/shard_map/all_to_all | solution.py:102
  7.5 0.0 copy-done
  7.5 0.7 fusion.34
  8.3 13.7 %all-to-all-done = bf16[1,2,512,512]{3,1,0,2:T(2,128)(2,1)S(1)} async-done(((bf16[1,2,512,512]{3,1,0,2:T(2,128)(2,1)}), bf16[1,2,512,512]{3,1,0,2:T(2,128)(2,1)S(1)}, u32[]{:S(2)}, u32[]{:S(2)}) %all-to-all-start) | async-done | bytes 1048608 | tf_op jit(solution)/shard_map/all_to_all | solution.py:102
  22.0 1.1 copy.52
  23.0 0.0 copy-start.1
  23.1 0.8 all_to_all.22
  23.8 0.1 dynamic-slice_bitcast_fusion
  23.9 1.9 %collective-permute-start = (bf16[1,2,128,1024]{3,2,1,0:T(8,128)(2,1)S(1)}, bf16[1,2,128,1024]{3,2,1,0:T(8,128)(2,1)S(1)}, u32[]{:S(2)}, u32[]{:S(2)}) collective-permute-start(bf16[1,2,128,1024]{3,2,1,0:T(8,128)(2,1)S(1)} %get-tuple-element.16), channel_id=1, source_target_pairs={{0,4},{4,0},{8,12},{12,8},{1,5},{5,1},{9,13},{13,9},{2,6},{6,2},{1... | collective-permute-start | bytes 1572872 | tf_op jit(solution)/shard_map/ppermute | solution.py:13
  25.8 1.4 maximum_bitcast_fusion
  29.6 0.0 copy-done.1
  29.6 0.0 copy-start.2
  29.7 0.1 broadcast_multiply_fusion.3
  29.8 7.3 %collective-permute-done = bf16[1,2,128,1024]{3,2,1,0:T(8,128)(2,1)S(1)} collective-permute-done((bf16[1,2,128,1024]{3,2,1,0:T(8,128)(2,1)S(1)}, bf16[1,2,128,1024]{3,2,1,0:T(8,128)(2,1)S(1)}, u32[]{:S(2)}, u32[]{:S(2)}) %collective-permute-start) | collective-permute-done | bytes 524320 | tf_op jit(solution)/shard_map/ppermute | solution.py:13
  37.1 0.1 fusion.27
  37.2 0.0 copy-done.2
  37.2 1.3 convolution_bitcast_fusion.1
  38.5 8.0 %fusion.22 = (f32[2,1,1,128,1024]{4,3,2,0,1:T(8,128)S(1)}, f32[2,1,1,128,1024]{4,3,2,0,1:T(8,128)S(1)}, f32[2,1,1,128,1024]{4,3,2,0,1:T(8,128)S(1)}, f32[2,1,1,128,1024]{4,3,2,0,1:T(8,128)S(1)}) fusion(f32[2,1,2,128,1024]{4,3,2,0,1:T(8,128)S(1)} %fusion.27, f32[2]{0:T(128)S(1)} %maximum_bitcast_fusion, f32[128,1024]{1,0:T(8,128)S(1)} %get-tuple-element.29, ...), kind=kLoop, calls=%fused_computation.37 | loop fusion | flops 3670016 | bytes 9437192 | tf_op jit(solution)/shard_map/sub | solution.py:37
  46.5 0.1 maximum_reduce_fusion
  46.7 0.1 maximum_reduce_fusion.1
  46.8 0.1 pad_maximum_fusion.1
  46.9 0.8 copy.36
  47.7 0.6 constant_dynamic-slice_fusion.1
  48.4 1.1 copy.48
  49.5 2.6 %collective-permute-start.1 = (bf16[1,2,64,2048]{3,2,1,0:T(8,128)(2,1)}, bf16[1,2,64,2048]{3,2,1,0:T(8,128)(2,1)S(1)}, u32[]{:S(2)}, u32[]{:S(2)}) collective-permute-start(bf16[1,2,64,2048]{3,2,1,0:T(8,128)(2,1)} %copy.48), channel_id=1, source_target_pairs={{0,8},{4,12},{8,0},{12,4},{1,9},{5,13},{9,1},{13,5},{2,10},{6,14},... | collective-permute-start | bytes 1572872 | tf_op jit(solution)/shard_map/ppermute | solution.py:13
  52.1 0.1 maximum_bitcast_fusion.1
  52.1 0.1 reshape.414
  52.2 0.2 broadcast_multiply_fusion.1
  52.4 0.3 copy.37
  52.7 21.4 %collective-permute-done.1 = bf16[1,2,64,2048]{3,2,1,0:T(8,128)(2,1)S(1)} collective-permute-done((bf16[1,2,64,2048]{3,2,1,0:T(8,128)(2,1)}, bf16[1,2,64,2048]{3,2,1,0:T(8,128)(2,1)S(1)}, u32[]{:S(2)}, u32[]{:S(2)}) %collective-permute-start.1) | collective-permute-done | bytes 524320 | tf_op jit(solution)/shard_map/ppermute | solution.py:13
  74.1 0.1 fusion.26
  74.2 5.7 %convolution_bitcast_fusion = f32[2,1,2,64,2048]{4,3,2,0,1:T(8,128)S(1)} fusion(bf16[2048,2048,1,1]{1,0,3,2:T(8,128)(2,1)} %constant.110, bf16[1,1,2,64,2048]{4,3,2,0,1:T(8,128)(2,1)S(1)} %bitcast.84, bf16[1,1,2,64,2048]{4,3,2,0,1:T(8,128)(2,1)S(1)} %bitcast.76), kind=kOutput, calls=%fused_computation.1 | convolution fusion | flops 2148007936 | bytes 11534336 | tf_op jit(solution)/shard_map/dot_general | solution.py:53
  80.0 8.0 %fusion.18 = (f32[2,1,1,64,2048]{4,3,2,0,1:T(8,128)S(1)}, f32[2,1,1,64,2048]{4,3,2,0,1:T(8,128)S(1)}, f32[2,1,1,64,2048]{4,3,2,0,1:T(8,128)S(1)}, f32[2,1,1,64,2048]{4,3,2,0,1:T(8,128)S(1)}) fusion(f32[2,1,2,64,2048]{4,3,2,0,1:T(8,128)S(1)} %fusion.26, f32[2]{0:T(128)S(1)} %maximum_bitcast_fusion.1, f32[64,2048]{1,0:T(8,128)S(1)} %get-tuple-element.19, ...), kind=kLoop, calls=%fused_computation.33 | loop fusion | flops 3670016 | bytes 9437192 | tf_op jit(solution)/shard_map/sub | solution.py:37
  88.0 0.1 maximum_reduce_fusion.2
  88.1 0.1 maximum_reduce_fusion.3
  88.2 0.1 pad_maximum_fusion.3
  88.3 1.5 %copy.39 = bf16[1,2,64,2048,2]{2,4,3,1,0:T(2,128)(2,1)S(1)} copy(bf16[1,2,64,2048,2]{3,2,1,4,0:T(8,128)(2,1)S(1)} %pad_maximum_fusion.3) | data formatting | bytes 2097152 | tf_op jit(solution)/shard_map/stack | solution.py:48
  89.8 0.8 copy.40
  90.7 0.6 gather_fusion
  91.3 0.1 copy.51
  91.4 30.2 %all_to_all.28 = bf16[4,2,1,2,512,64]{4,5,3,2,1,0:T(8,128)(2,1)S(1)} all-to-all(bf16[4,2,1,2,512,64]{4,5,3,2,1,0:T(8,128)(2,1)S(1)} %bitcast.72), channel_id=1, replica_groups=mesh['swath'=2,'sub'=4,'beam'=2,'half'=2] {'sub'}, dimensions={0} | all-to-all | bytes 2097152 | tf_op jit(solution)/shard_map/all_to_all | solution.py:120
  121.6 0.1 copy.42
  121.7 15.6 %all_to_all.29 = bf16[4,2,1,2,512,64]{4,5,3,2,0,1:T(8,128)(2,1)S(1)} all-to-all(bf16[4,2,1,2,512,64]{4,5,3,2,0,1:T(8,128)(2,1)S(1)} %copy.42), channel_id=1, replica_groups=mesh['swath'=2,'sub'=4,'beam'=2,'half'=2] {'beam'}, dimensions={1} | all-to-all | bytes 2097152 | tf_op jit(solution)/shard_map/all_to_all | solution.py:119
  137.3 0.1 copy.43
  137.4 0.1 copy.44
  137.5 1.3 copy.45
  (5 shorter events, 0.0 us)
Async XLA Ops:
  0.0 7.5 %copy-start = (f32[4]{0:T(128)S(1)}, f32[4]{0:T(128)}, u32[]{:S(2)}) copy-start(f32[4]{0:T(128)} %param.6) | copy-start | bytes 52
  3.3 18.7 %all-to-all-start = ((bf16[1,2,512,512]{3,1,0,2:T(2,128)(2,1)}), bf16[1,2,512,512]{3,1,0,2:T(2,128)(2,1)S(1)}, u32[]{:S(2)}, u32[]{:S(2)}) async-start(bf16[1,2,512,512]{3,1,0,2:T(2,128)(2,1)} %copy.34), calls=%async_computation | async-start | bytes 2097152 | tf_op jit(solution)/shard_map/all_to_all | solution.py:102
  23.0 6.6 %copy-start.1 = (s32[2,4]{1,0:T(2,128)S(1)}, s32[2,4]{1,0:T(2,128)}, u32[]{:S(2)}) copy-start(s32[2,4]{1,0:T(2,128)} %param.7) | copy-start | bytes 100
  23.9 13.2 %collective-permute-start = (bf16[1,2,128,1024]{3,2,1,0:T(8,128)(2,1)S(1)}, bf16[1,2,128,1024]{3,2,1,0:T(8,128)(2,1)S(1)}, u32[]{:S(2)}, u32[]{:S(2)}) collective-permute-start(bf16[1,2,128,1024]{3,2,1,0:T(8,128)(2,1)S(1)} %get-tuple-element.16), channel_id=1, source_target_pairs={{0,4},{4,0},{8,12},{12,8},{1,5},{5,1},{9,13},{13,9},{2,6},{6,2},{1... | collective-permute-start | bytes 1572872 | tf_op jit(solution)/shard_map/ppermute | solution.py:13
  29.6 7.6 %copy-start.2 = (bf16[1024,1024,1,1]{1,0,3,2:T(8,128)(2,1)S(1)}, bf16[1024,1024,1,1]{1,0,3,2:T(8,128)(2,1)}, u32[]{:S(2)}) copy-start(bf16[1024,1024,1,1]{1,0,3,2:T(8,128)(2,1)} %constant.109) | copy-start | bytes 6291460
  49.5 24.6 %collective-permute-start.1 = (bf16[1,2,64,2048]{3,2,1,0:T(8,128)(2,1)}, bf16[1,2,64,2048]{3,2,1,0:T(8,128)(2,1)S(1)}, u32[]{:S(2)}, u32[]{:S(2)}) collective-permute-start(bf16[1,2,64,2048]{3,2,1,0:T(8,128)(2,1)} %copy.48), channel_id=1, source_target_pairs={{0,8},{4,12},{8,0},{12,4},{1,9},{5,13},{9,1},{13,5},{2,10},{6,14},... | collective-permute-start | bytes 1572872 | tf_op jit(solution)/shard_map/ppermute | solution.py:13
where the time goes:
time: 139 us
  blocking collectives  45.8 us (33%)
  waiting for transfers between devices  42.3 us (30%)
  other arithmetic  18.8 us (14%)
  local copies, waits for them, and re-layouts  13.5 us (10%)
  starting transfers between devices  8.68 us (6%)
  matrix products  7.03 us (5%)
  between operations  2.69 us (2%)
    all_to_all x1, blocking collectives, body(): lax.all_to_all(outgoing, 'sub', split_axis=0, concat_axis=0, tiled=True)  30.2 us
    ppermute x2, waiting for transfers between devices, swapped(): lax.ppermute(value, axis, [(i, i ^ 1 << distance) for i in range(lax.axis...  28.6 us
    sub x2, other arithmetic, steer_phase(): real_part * cosine - imag_part * sines  16 us
    all_to_all x1, blocking collectives, body(): lax.all_to_all(lax.all_to_all(outgoing, 'sub', split_axis=0, concat_axis=...  15.6 us
    all_to_all x1, waiting for transfers between devices, body(): lax.all_to_all(images, 'beam', split_axis=2, concat_axis=3, tiled=True)  13.7 us
    dot_general x2, matrix products, odd_local(): jnp.dot(children.reshape(-1, children.shape[-1]), kernel, preferred_eleme...  7.03 us
    ppermute x2, starting transfers between devices, swapped(): lax.ppermute(value, axis, [(i, i ^ 1 << distance) for i in range(lax.axis...  4.45 us
    unnamed x8, local copies, waits for them, and re-layouts  4.43 us
  transfers between devices with their start and end apart: 3, of which 3 were waited for; matrix products, arithmetic and copies ran while one was open for 2% of the time, Pallas kernels for 0%

commit v1 on v0

--- a/solution.py
+++ b/solution.py
@@ -1,3 +1,4 @@
+import functools
 import math
 import jax
 import numpy as np
@@ -7,6 +8,32 @@
 
 B = 1024
 NR = 1024
+
+
+def local_data_tell(local_x, comm_axis):
+    built, f_now = (lax.axis_size(comm_axis), lax.axis_index(comm_axis))
+    s_next = local_x.shape[0] // built
+    o_now = list(local_x.shape)
+    o_now[0] = s_next
+    u_next = o_now[0]
+    o_now[0] = u_next * built
+    val2 = jnp.zeros(o_now, local_x.dtype)
+    dev_i = 0
+    while dev_i < built:
+        e_now = lax.dynamic_slice_in_dim(local_x, (f_now ^ dev_i) * s_next, s_next, axis=0)
+        if dev_i:
+            steps_seen = []
+            ix = 0
+            while ix < built:
+                steps_seen.append((ix, ix ^ dev_i))
+                ix = ix + 1
+            e_now = lax.ppermute(e_now, comm_axis, steps_seen)
+        val2 = lax.dynamic_update_slice_in_dim(val2, e_now, (f_now ^ dev_i) * u_next, axis=0)
+        dev_i = dev_i + 1
+    return val2
+
+
+search_the_sections = functools.partial(local_data_tell, comm_axis="sub")
 
 
 def swapped(value, axis, distance):
@@ -117,11 +144,7 @@
     picked = sector_tiles[:, :, :, beam_ids, owners, :]
     outgoing = picked.transpose(4, 3, 0, 1, 5, 2)
     received = lax.all_to_all(
-        lax.all_to_all(outgoing, "sub", split_axis=0, concat_axis=0, tiled=True),
-        "beam",
-        split_axis=1,
-        concat_axis=1,
-        tiled=True,
+        search_the_sections(outgoing), "beam", split_axis=1, concat_axis=1, tiled=True
     )
     sector_width = received.shape[4]
     received = received.reshape(

time: 139 us -> 134 us (0.964)
  the two profiles are of different devices: /device:TPU:0 before, /device:TPU:12 now
where the time goes in v1:
time: 134 us; the launch traced here: 133 us
  waiting for transfers between devices  64.5 us (48%)
  other arithmetic  18.7 us (14%)
  blocking collectives  15.7 us (12%)
  local copies, waits for them, and re-layouts  13.8 us (10%)
  starting transfers between devices  10.7 us (8%)
  matrix products  7.03 us (5%)
  between operations  2.95 us (2%)
    ppermute x2, waiting for transfers between devices, swapped(): lax.ppermute(value, axis, [(i, i ^ 1 << distance) for i in range(lax.axis...  28.6 us
    ppermute x3, waiting for transfers between devices, local_data_tell(): e_now = lax.ppermute(e_now, comm_axis, steps_seen)  22.8 us
    sub x2, other arithmetic, steer_phase(): real_part * cosine - imag_part * sines  16 us
    all_to_all x1, blocking collectives, body(): lax.all_to_all(search_the_sections(outgoing), 'beam', split_axis=1, conca...  15.7 us
    all_to_all x1, waiting for transfers between devices, body(): lax.all_to_all(images, 'beam', split_axis=2, concat_axis=3, tiled=True)  13 us
    dot_general x2, matrix products, odd_local(): jnp.dot(children.reshape(-1, children.shape[-1]), kernel, preferred_eleme...  7.03 us
    unnamed x8, local copies, waits for them, and re-layouts  4.43 us
    ppermute x3, starting transfers between devices, local_data_tell(): e_now = lax.ppermute(e_now, comm_axis, steps_seen)  3.97 us
  transfers between devices with their start and end apart: 6, of which 6 were waited for; matrix products, arithmetic and copies ran while one was open for 2% of the time, Pallas kernels for 0%

profile of v1, /device:TPU:12, one launch (start us, length us, event | category | flops | bytes accessed | tf_op | source)
XLA Modules:
  0.0 133.2 jit_solution(13610771215091737297)
XLA Ops:
  0.0 0.0 copy-start
  0.0 3.3 %copy.33 = bf16[1,2,512,512]{3,1,0,2:T(2,128)(2,1)} copy(bf16[1,2,512,512]{3,2,1,0:T(8,128)(2,1)} %param.5) | data formatting | bytes 2097152 | tf_op args[0]
  3.3 3.6 %all-to-all-start = ((bf16[1,2,512,512]{3,1,0,2:T(2,128)(2,1)}), bf16[1,2,512,512]{3,1,0,2:T(2,128)(2,1)S(1)}, u32[]{:S(2)}, u32[]{:S(2)}) async-start(bf16[1,2,512,512]{3,1,0,2:T(2,128)(2,1)} %copy.33), calls=%async_computation | async-start | bytes 2097152 | tf_op jit(solution)/shard_map/all_to_all | solution.py:129
  7.0 0.0 copy-done
  7.0 0.7 fusion.34
  7.7 13.0 %all-to-all-done = bf16[1,2,512,512]{3,1,0,2:T(2,128)(2,1)S(1)} async-done(((bf16[1,2,512,512]{3,1,0,2:T(2,128)(2,1)}), bf16[1,2,512,512]{3,1,0,2:T(2,128)(2,1)S(1)}, u32[]{:S(2)}, u32[]{:S(2)}) %all-to-all-start) | async-done | bytes 1048608 | tf_op jit(solution)/shard_map/all_to_all | solution.py:129
  20.7 1.1 copy.51
  21.8 0.0 copy-start.1
  21.8 0.9 all_to_all.19
  22.8 0.1 dynamic-slice_bitcast_fusion
  22.9 0.5 collective-permute-start
  23.4 1.3 maximum_bitcast_fusion
  27.2 0.0 copy-done.1
  27.2 0.0 copy-start.2
  27.3 0.1 broadcast_multiply_fusion.3
  27.4 8.3 %collective-permute-done = bf16[1,2,128,1024]{3,2,1,0:T(8,128)(2,1)S(1)} collective-permute-done((bf16[1,2,128,1024]{3,2,1,0:T(8,128)(2,1)S(1)}, bf16[1,2,128,1024]{3,2,1,0:T(8,128)(2,1)S(1)}, u32[]{:S(2)}, u32[]{:S(2)}) %collective-permute-start) | collective-permute-done | bytes 524320 | tf_op jit(solution)/shard_map/ppermute | solution.py:40
  35.7 0.1 fusion.27
  35.9 0.0 copy-done.2
  35.9 1.3 convolution_bitcast_fusion.1
  37.2 8.0 %fusion.22 = (f32[2,1,1,128,1024]{4,3,2,0,1:T(8,128)S(1)}, f32[2,1,1,128,1024]{4,3,2,0,1:T(8,128)S(1)}, f32[2,1,1,128,1024]{4,3,2,0,1:T(8,128)S(1)}, f32[2,1,1,128,1024]{4,3,2,0,1:T(8,128)S(1)}) fusion(f32[2,1,2,128,1024]{4,3,2,0,1:T(8,128)S(1)} %fusion.27, f32[2]{0:T(128)S(1)} %maximum_bitcast_fusion, f32[128,1024]{1,0:T(8,128)S(1)} %get-tuple-element.32, ...), kind=kLoop, calls=%fused_computation.37 | loop fusion | flops 3670016 | bytes 9437192 | tf_op jit(solution)/shard_map/sub | solution.py:64
  45.2 0.1 maximum_reduce_fusion
  45.3 0.1 maximum_reduce_fusion.1
  45.5 0.1 pad_maximum_fusion.1
  45.6 0.8 copy.35
  46.4 0.6 constant_dynamic-slice_fusion.1
  47.0 1.1 copy.49
  48.2 2.6 %collective-permute-start.1 = (bf16[1,2,64,2048]{3,2,1,0:T(8,128)(2,1)}, bf16[1,2,64,2048]{3,2,1,0:T(8,128)(2,1)S(1)}, u32[]{:S(2)}, u32[]{:S(2)}) collective-permute-start(bf16[1,2,64,2048]{3,2,1,0:T(8,128)(2,1)} %copy.49), channel_id=1, source_target_pairs={{0,8},{4,12},{8,0},{12,4},{1,9},{5,13},{9,1},{13,5},{2,10},{6,14},... | collective-permute-start | bytes 1572872 | tf_op jit(solution)/shard_map/ppermute | solution.py:40
  50.8 0.1 maximum_bitcast_fusion.1
  50.8 0.1 reshape.414
  50.9 0.2 broadcast_multiply_fusion.1
  51.1 0.3 copy.36
  51.4 20.3 %collective-permute-done.1 = bf16[1,2,64,2048]{3,2,1,0:T(8,128)(2,1)S(1)} collective-permute-done((bf16[1,2,64,2048]{3,2,1,0:T(8,128)(2,1)}, bf16[1,2,64,2048]{3,2,1,0:T(8,128)(2,1)S(1)}, u32[]{:S(2)}, u32[]{:S(2)}) %collective-permute-start.1) | collective-permute-done | bytes 524320 | tf_op jit(solution)/shard_map/ppermute | solution.py:40
  71.7 0.1 fusion.26
  71.8 5.7 %convolution_bitcast_fusion = f32[2,1,2,64,2048]{4,3,2,0,1:T(8,128)S(1)} fusion(bf16[2048,2048,1,1]{1,0,3,2:T(8,128)(2,1)} %constant.114, bf16[1,1,2,64,2048]{4,3,2,0,1:T(8,128)(2,1)S(1)} %bitcast.109, bf16[1,1,2,64,2048]{4,3,2,0,1:T(8,128)(2,1)S(1)} %bitcast.101), kind=kOutput, calls=%fused_computation.1 | convolution fusion | flops 2148007936 | bytes 11534336 | tf_op jit(solution)/shard_map/dot_general | solution.py:80
  77.6 8.0 %fusion.18 = (f32[2,1,1,64,2048]{4,3,2,0,1:T(8,128)S(1)}, f32[2,1,1,64,2048]{4,3,2,0,1:T(8,128)S(1)}, f32[2,1,1,64,2048]{4,3,2,0,1:T(8,128)S(1)}, f32[2,1,1,64,2048]{4,3,2,0,1:T(8,128)S(1)}) fusion(f32[2,1,2,64,2048]{4,3,2,0,1:T(8,128)S(1)} %fusion.26, f32[2]{0:T(128)S(1)} %maximum_bitcast_fusion.1, f32[64,2048]{1,0:T(8,128)S(1)} %get-tuple-element.22, ...), kind=kLoop, calls=%fused_computation.33 | loop fusion | flops 3670016 | bytes 9437192 | tf_op jit(solution)/shard_map/sub | solution.py:64
  85.6 0.1 maximum_reduce_fusion.2
  85.7 0.1 maximum_reduce_fusion.3
  85.8 0.1 pad_maximum_fusion.3
  85.9 1.5 %copy.38 = bf16[1,2,64,2048,2]{2,4,3,1,0:T(2,128)(2,1)S(1)} copy(bf16[1,2,64,2048,2]{3,2,1,4,0:T(8,128)(2,1)S(1)} %pad_maximum_fusion.3) | data formatting | bytes 2097152 | tf_op jit(solution)/shard_map/stack | solution.py:75
  87.4 0.8 copy.39
  88.3 0.6 gather_fusion
  88.9 0.1 dynamic-slice_bitcast_fusion.1
  89.0 1.3 collective-permute-start.2
  90.3 2.1 %collective-permute-start.3 = (bf16[1,2,1,2,512,64]{4,5,3,1,0,2:T(8,128)(2,1)S(1)}, bf16[1,2,1,2,512,64]{4,5,3,1,0,2:T(8,128)(2,1)S(1)}, u32[]{:S(2)}, u32[]{:S(2)}) collective-permute-start(bf16[1,2,1,2,512,64]{4,5,3,1,0,2:T(8,128)(2,1)S(1)} %get-tuple-element.14), channel_id=1, source_target_pairs={{0,8},{4,12},{8,0},{12,4},{1,9},{5,13},{9,1},{13,5},{2,10},{6,14},... | collective-permute-start | bytes 786440 | tf_op jit(solution)/shard_map/ppermute | solution.py:30
  92.4 0.1 broadcast_in_dim.6
  92.6 0.6 collective-permute-start.4
  93.1 7.0 %collective-permute-done.2 = bf16[1,2,1,2,512,64]{4,5,3,1,0,2:T(8,128)(2,1)S(1)} collective-permute-done((bf16[1,2,1,2,512,64]{4,5,3,1,0,2:T(8,128)(2,1)S(1)}, bf16[1,2,1,2,512,64]{4,5,3,1,0,2:T(8,128)(2,1)S(1)}, u32[]{:S(2)}, u32[]{:S(2)}) %collective-permute-start.2) | collective-permute-done | bytes 262176 | tf_op jit(solution)/shard_map/ppermute | solution.py:30
  100.2 10.2 %collective-permute-done.3 = bf16[1,2,1,2,512,64]{4,5,3,1,0,2:T(8,128)(2,1)S(1)} collective-permute-done((bf16[1,2,1,2,512,64]{4,5,3,1,0,2:T(8,128)(2,1)S(1)}, bf16[1,2,1,2,512,64]{4,5,3,1,0,2:T(8,128)(2,1)S(1)}, u32[]{:S(2)}, u32[]{:S(2)}) %collective-permute-start.3) | collective-permute-done | bytes 262176 | tf_op jit(solution)/shard_map/ppermute | solution.py:30
  110.4 5.6 %collective-permute-done.4 = bf16[1,2,1,2,512,64]{4,5,3,1,0,2:T(8,128)(2,1)S(1)} collective-permute-done((bf16[1,2,1,2,512,64]{4,5,3,1,0,2:T(8,128)(2,1)S(1)}, bf16[1,2,1,2,512,64]{4,5,3,1,0,2:T(8,128)(2,1)S(1)}, u32[]{:S(2)}, u32[]{:S(2)}) %collective-permute-start.4) | collective-permute-done | bytes 262176 | tf_op jit(solution)/shard_map/ppermute | solution.py:30
  116.0 15.7 %all_to_all.23 = bf16[4,2,1,2,512,64]{4,5,3,2,0,1:T(8,128)(2,1)S(1)} all-to-all(bf16[4,2,1,2,512,64]{4,5,3,2,0,1:T(8,128)(2,1)S(1)} %bitcast_dynamic-update-slice_fusion.1), channel_id=1, replica_groups=mesh['swath'=2,'sub'=4,'beam'=2,'half'=2] {'beam'}, dimensions={1} | all-to-all | bytes 2097152 | tf_op jit(solution)/shard_map/all_to_all | solution.py:146
  131.7 0.1 copy.44
  131.8 0.1 copy.45
  131.9 1.3 copy.46
  (9 shorter events, 0.1 us)
Async XLA Ops:
  0.0 7.0 %copy-start = (f32[4]{0:T(128)S(1)}, f32[4]{0:T(128)}, u32[]{:S(2)}) copy-start(f32[4]{0:T(128)} %param.6) | copy-start | bytes 52
  3.3 17.4 %all-to-all-start = ((bf16[1,2,512,512]{3,1,0,2:T(2,128)(2,1)}), bf16[1,2,512,512]{3,1,0,2:T(2,128)(2,1)S(1)}, u32[]{:S(2)}, u32[]{:S(2)}) async-start(bf16[1,2,512,512]{3,1,0,2:T(2,128)(2,1)} %copy.33), calls=%async_computation | async-start | bytes 2097152 | tf_op jit(solution)/shard_map/all_to_all | solution.py:129
  21.8 5.4 %copy-start.1 = (s32[2,4]{1,0:T(2,128)S(1)}, s32[2,4]{1,0:T(2,128)}, u32[]{:S(2)}) copy-start(s32[2,4]{1,0:T(2,128)} %param.7) | copy-start | bytes 100
  22.9 12.9 %collective-permute-start = (bf16[1,2,128,1024]{3,2,1,0:T(8,128)(2,1)S(1)}, bf16[1,2,128,1024]{3,2,1,0:T(8,128)(2,1)S(1)}, u32[]{:S(2)}, u32[]{:S(2)}) collective-permute-start(bf16[1,2,128,1024]{3,2,1,0:T(8,128)(2,1)S(1)} %get-tuple-element.19), channel_id=1, source_target_pairs={{0,4},{4,0},{8,12},{12,8},{1,5},{5,1},{9,13},{13,9},{2,6},{6,2},{1... | collective-permute-start | bytes 1572872 | tf_op jit(solution)/shard_map/ppermute | solution.py:40
  27.2 8.6 %copy-start.2 = (bf16[1024,1024,1,1]{1,0,3,2:T(8,128)(2,1)S(1)}, bf16[1024,1024,1,1]{1,0,3,2:T(8,128)(2,1)}, u32[]{:S(2)}) copy-start(bf16[1024,1024,1,1]{1,0,3,2:T(8,128)(2,1)} %constant.113) | copy-start | bytes 6291460
  48.2 23.5 %collective-permute-start.1 = (bf16[1,2,64,2048]{3,2,1,0:T(8,128)(2,1)}, bf16[1,2,64,2048]{3,2,1,0:T(8,128)(2,1)S(1)}, u32[]{:S(2)}, u32[]{:S(2)}) collective-permute-start(bf16[1,2,64,2048]{3,2,1,0:T(8,128)(2,1)} %copy.49), channel_id=1, source_target_pairs={{0,8},{4,12},{8,0},{12,4},{1,9},{5,13},{9,1},{13,5},{2,10},{6,14},... | collective-permute-start | bytes 1572872 | tf_op jit(solution)/shard_map/ppermute | solution.py:40
  89.0 11.1 %collective-permute-start.2 = (bf16[1,2,1,2,512,64]{4,5,3,1,0,2:T(8,128)(2,1)S(1)}, bf16[1,2,1,2,512,64]{4,5,3,1,0,2:T(8,128)(2,1)S(1)}, u32[]{:S(2)}, u32[]{:S(2)}) collective-permute-start(bf16[1,2,1,2,512,64]{4,5,3,1,0,2:T(8,128)(2,1)S(1)} %get-tuple-element.15), channel_id=1, source_target_pairs={{0,4},{4,0},{8,12},{12,8},{1,5},{5,1},{9,13},{13,9},{2,6},{6,2},{1... | collective-permute-start | bytes 786440 | tf_op jit(solution)/shard_map/ppermute | solution.py:30
  90.3 20.1 %collective-permute-start.3 = (bf16[1,2,1,2,512,64]{4,5,3,1,0,2:T(8,128)(2,1)S(1)}, bf16[1,2,1,2,512,64]{4,5,3,1,0,2:T(8,128)(2,1)S(1)}, u32[]{:S(2)}, u32[]{:S(2)}) collective-permute-start(bf16[1,2,1,2,512,64]{4,5,3,1,0,2:T(8,128)(2,1)S(1)} %get-tuple-element.14), channel_id=1, source_target_pairs={{0,8},{4,12},{8,0},{12,4},{1,9},{5,13},{9,1},{13,5},{2,10},{6,14},... | collective-permute-start | bytes 786440 | tf_op jit(solution)/shard_map/ppermute | solution.py:30
  92.6 23.5 %collective-permute-start.4 = (bf16[1,2,1,2,512,64]{4,5,3,1,0,2:T(8,128)(2,1)S(1)}, bf16[1,2,1,2,512,64]{4,5,3,1,0,2:T(8,128)(2,1)S(1)}, u32[]{:S(2)}, u32[]{:S(2)}) collective-permute-start(bf16[1,2,1,2,512,64]{4,5,3,1,0,2:T(8,128)(2,1)S(1)} %get-tuple-element.13), channel_id=1, source_target_pairs={{0,12},{4,8},{8,4},{12,0},{1,13},{5,9},{9,5},{13,1},{2,14},{6,10},... | collective-permute-start | bytes 786440 | tf_op jit(solution)/shard_map/ppermute | solution.py:30
